TPU v7x, 256 devices: a whole 4x4x8 slice. The times are simulated.
256 devices in a mesh: dp: 8 (over y, core), seq: 32 (over x, z).
Axes of the slice: x: 4, y: 4, z: 8, core: 2. Of those that a mesh axis runs over, the one named last changes fastest.
Arguments:
- queries: bfloat16 [16, 2048, 1536], P('dp', 'seq'), may hold values from -6 to 6
- key_rows: bfloat16 [16, 2048, 1536], P('dp', 'seq'), may hold values from -6 to 6
- value_rows: bfloat16 [16, 2048, 1536], P('dp', 'seq'), may hold values from -6 to 6
- layer_input: bfloat16 [16, 2048, 1536], P('dp', 'seq'), may hold values from -6 to 6
- utt_lengths: int32 [16], P('dp'), may hold values from 512 to 2048, as said below
- out_weight: bfloat16 [1536, 1536], replicated, may hold values from -0.15625 to 0.15625
- conv_kernel: bfloat16 [31, 1536], replicated, may hold values from -1 to 1
- conv_cotangent: bfloat16 [16, 2048, 1536], P('dp', 'seq'), may hold values from -6 to 6
- pick_weight: int32 [23592], replicated, may hold values from 0 to 2359295
- pick_kernel: int32 [476], replicated, may hold values from 0 to 47615
Outputs:
- conv_out: bfloat16 [16, 2048, 1536], P('dp', 'seq')
- context_grad: bfloat16 [16, 2048, 1536], P('dp', 'seq')
- weight_picks: float32 [23592], replicated
- kernel_picks: float32 [476], replicated
Inputs may be any that keep to these rules, and one draw needn't show every extreme that they name: `utt_lengths`: the first utterance fills all 2048 slots and the last has 512 valid frames.
All inputs are finite; a program needn't handle non-finite values.
Results may differ from a plain program's by a relative error of at most 0.0056.
Values may be sent and summed in bfloat16 or wider, within the bound.
No kernel may reach another device: no remote copies, remote signals or barrier semaphores. Data moves between devices by JAX's collectives and lax.ppermute only.
A program may use at most 128 MiB of HBM per device.

v0:
```python
import math
import jax
import jax.numpy as jnp
from jax import lax
from jax.sharding import PartitionSpec as P

HEADS = 16
neg_big = -1e30


def padded(value, sides, width):
    for axis, dim in sides:
        count, length = (lax.axis_size(axis), value.shape[dim])
        up = [(i, (i + 1) % count) for i in range(count - 1)]
        down = [(j, i) for i, j in up]
        last = lax.slice_in_dim(value, length - width, length, axis=dim)
        leading = lax.slice_in_dim(value, 0, width, axis=dim)
        before = lax.ppermute(last, axis, up)
        after = lax.ppermute(leading, axis, down)
        value = jnp.concatenate([before, value, after], axis=dim)
    return value


def softmax_rows(scores, key_ok):
    scores = jnp.where(key_ok, scores, neg_big)
    row_max = jnp.max(scores, axis=-1, keepdims=True)
    probs = jnp.exp(scores - row_max)
    return (probs.astype(jnp.bfloat16), jnp.sum(probs, axis=-1))


def pick_entries(table, picks):
    flat = table.reshape(-1)
    lane = math.gcd(flat.shape[0], 128)
    blocks = flat.reshape(flat.shape[0] // lane, lane)
    chosen = jnp.take(blocks, picks // lane, axis=0)
    lane_ids = jnp.arange(lane, dtype=jnp.int32)
    hit = lane_ids[None, :] == (picks % lane)[:, None]
    return jnp.sum(jnp.where(hit, chosen, jnp.float32(0.0)), axis=1)


def on_device(
    queries,
    key_rows,
    value_rows,
    layer_input,
    utt_lengths,
    out_weight,
    conv_kernel,
    conv_cotangent,
    pick_weight,
    pick_kernel,
):
    local_utts, frames_dev, width = queries.shape
    seq_count = lax.axis_size("seq")
    full_frames = frames_dev * seq_count
    head_size = width // HEADS
    score_scale = 1.0 / math.sqrt(head_size)
    first_frame = lax.axis_index("seq") * frames_dev
    local_ids = first_frame + jnp.arange(frames_dev, dtype=jnp.int32)
    valid_rows = (local_ids[None, :] < utt_lengths[:, None]).astype(jnp.float32)
    all_keys, all_values = (
        lax.all_gather(key_rows, "seq", axis=1, tiled=True),
        lax.all_gather(value_rows, "seq", axis=1, tiled=True),
    )
    full_ids = jnp.arange(full_frames, dtype=jnp.int32)

    def one_utt(item):
        query_utt, key_utt, value_utt, length_utt = item
        query_heads = query_utt.reshape(frames_dev, HEADS, head_size)
        key_heads = key_utt.reshape(full_frames, HEADS, head_size)
        value_heads = value_utt.reshape(full_frames, HEADS, head_size)
        scores = (
            jnp.einsum("qhd,khd->hqk", query_heads, key_heads, preferred_element_type=jnp.float32)
            * score_scale
        )
        weights, denom = softmax_rows(scores, (full_ids < length_utt)[None, None, :])
        out_rows = jnp.einsum(
            "hqk,khd->qhd", weights, value_heads, preferred_element_type=jnp.float32
        )
        out_rows = out_rows / denom.transpose(1, 0)[:, :, None]
        return out_rows.astype(jnp.bfloat16).reshape(frames_dev, width)

    context = lax.map(one_utt, (queries, all_keys, all_values, utt_lengths))
    context_flat = context.reshape(local_utts * frames_dev, width)
    projected = jnp.dot(context_flat, out_weight, preferred_element_type=jnp.float32).reshape(
        local_utts, frames_dev, width
    )
    hidden = ((layer_input.astype(jnp.float32) + projected) * valid_rows[:, :, None]).astype(
        jnp.bfloat16
    )
    tap_count = conv_kernel.shape[0]
    half_taps = (tap_count - 1) // 2
    kernel_f = conv_kernel.astype(jnp.float32)
    hidden_pad = padded(hidden, (("seq", 1),), half_taps)
    cot_f = conv_cotangent.astype(jnp.float32)
    conv_sum = jnp.zeros((local_utts, frames_dev, width), jnp.float32)
    kernel_rows = []
    for offset in range(tap_count):
        window = hidden_pad[:, offset : offset + frames_dev].astype(jnp.float32)
        conv_sum = conv_sum + kernel_f[offset] * window
        kernel_rows.append(jnp.sum(window * cot_f, axis=(0, 1)))
    conv_out = conv_sum.astype(jnp.bfloat16)
    kernel_grad = jnp.stack(kernel_rows)
    cot_pad = padded(conv_cotangent, (("seq", 1),), half_taps).astype(jnp.float32)
    back_sum = jnp.zeros((local_utts, frames_dev, width), jnp.float32)
    for offset in range(tap_count):
        begin = 2 * half_taps - offset
        back_sum = back_sum + kernel_f[offset] * cot_pad[:, begin : begin + frames_dev]
    hidden_grad = (back_sum * valid_rows[:, :, None]).astype(jnp.bfloat16)
    grad_flat = hidden_grad.reshape(local_utts * frames_dev, width)
    weight_grad = lax.dot_general(
        context_flat, grad_flat, (((0,), (0,)), ((), ())), preferred_element_type=jnp.float32
    )
    context_grad = lax.dot_general(
        grad_flat, out_weight, (((1,), (1,)), ((), ())), preferred_element_type=jnp.float32
    )
    context_grad = context_grad.reshape(local_utts, frames_dev, width).astype(jnp.bfloat16)
    weight_vals = pick_entries(weight_grad, pick_weight)
    kernel_vals = pick_entries(kernel_grad, pick_kernel)
    weight_sum, kernel_sum = lax.psum((weight_vals, kernel_vals), ("dp", "seq"))
    total_slots = local_utts * lax.axis_size("dp") * full_frames
    norm_factor = 1.0 / math.sqrt(total_slots)
    return (conv_out, context_grad, weight_sum * norm_factor, kernel_sum * norm_factor)


def solution(mesh):
    placed = (
        P("dp", "seq", None),
        P("dp", "seq", None),
        P("dp", "seq", None),
        P("dp", "seq", None),
        P("dp"),
        P(),
        P(),
        P("dp", "seq", None),
        P(),
        P(),
    )
    return jax.shard_map(
        on_device,
        mesh=mesh,
        in_specs=placed,
        out_specs=(P("dp", "seq", None), P("dp", "seq", None), P(), P()),
        check_vma=False,
    )
```

profile of v0, /device:TPU:1, one launch (start us, length us, event | category | flops | bytes accessed | tf_op | source)
XLA Modules:
  0.0 756.6 jit_solution(8033392045944065864)
XLA Ops:
  7.2 0.0 all-gather.3.cloned.1.call-start
  7.2 2.1 copy.22
  9.4 0.0 all-gather.3.cloned.1.call-update
  9.4 0.0 all-gather.5.cloned.1.call-start
  9.4 2.2 copy.23
  11.6 0.0 all-gather.5.cloned.1.call-update
  11.6 0.0 all-reduce.2.cloned.1.call-start
  11.7 1.0 fusion.165
  12.6 4.4 collective-permute-start.2
  17.0 1.3 collective-permute-start.3
  18.3 0.9 convert_element_type.130
  19.3 0.2 slice_reduce_fusion.29
  19.6 0.3 slice_reduce_fusion.30
  20.1 0.7 compare_convert_fusion
  20.8 1.3 add_select_fusion.3
  22.1 1.3 compare_and_fusion.1
  23.4 1.6 compare_and_fusion
  25.0 1.6 add_select_fusion.1
  26.6 0.6 pad_clamp_fusion.1
  27.2 1.3 maximum_convert_fusion
  28.5 3.3 fusion.104
  32.1 2.4 fusion.34
  34.5 99.7 %all-gather.3.cloned.1.call-done = bf16[2,2048,1536]{2,0,1:T(2,128)(2,1)} async-done(((bf16[2,64,1536]{2,0,1:T(2,128)(2,1)}), bf16[2,2048,1536]{2,0,1:T(2,128)(2,1)}) %all-gather.3.cloned.1.call-update) | async-done | bytes 12582928 | tf_op jit(solution)/shard_map/all_gather | solution.py:63
  134.2 31.1 %copy.24 = bf16[2,2048,1536]{1,2,0:T(8,128)(2,1)} copy(bf16[2,2048,1536]{2,0,1:T(2,128)(2,1)} %all-gather.3.cloned.1.call-done) | data formatting | bytes 25165824
  165.4 88.2 %all-gather.5.cloned.1.call-done = bf16[2,2048,1536]{2,0,1:T(2,128)(2,1)} async-done(((bf16[2,64,1536]{2,0,1:T(2,128)(2,1)}), bf16[2,2048,1536]{2,0,1:T(2,128)(2,1)}) %all-gather.5.cloned.1.call-update) | async-done | bytes 12582928 | tf_op jit(solution)/shard_map/all_gather | solution.py:62
  253.6 31.1 %copy.25 = bf16[2,2048,1536]{1,2,0:T(8,128)(2,1)} copy(bf16[2,2048,1536]{2,0,1:T(2,128)(2,1)} %all-gather.5.cloned.1.call-done) | data formatting | bytes 25165824
  284.7 51.8 %while.11 = (s32[]{:T(128)}, bf16[2,64,1536]{2,1,0:T(8,128)(2,1)S(1)}, bf16[2,2048,1536]{1,2,0:T(8,128)(2,1)}, s32[2]{0:T(128)S(1)}, bf16[2,64,1536]{2,1,0:T(8,1...) while((s32[]{:T(128)}, bf16[2,64,1536]{2,1,0:T(8,128)(2,1)S(1)}, ...), condition=%wide.region_3.4_spmd.clone, body=%wide.region_0.3_spmd.clone.sunk | while | flops 828571648 | bytes 65302632 | solution.py:83
  284.7 11.9 %constant_dynamic-slice_fusion.5 = (bf16[1,2048,1536]{1,2,0:T(8,128)(2,1)}, bf16[1,2048,1536]{1,2,0:T(8,128)(2,1)}) fusion(bf16[2,2048,1536]{1,2,0:T(8,128)(2,1)} %get-tuple-element.212, s32[]{:T(128)} %get-tuple-element.200, bf16[2,2048,1536]{1,2,0:T(8,128)(2,1)} %get-tuple-element.209), kind=kLoop, calls=%fused_computation.20.clone.1 | loop fusion | bytes 25165828 | tf_op jit(solution)/shard_map/while/body/jit(dynamic_index_in_dim)/dynamic_slice | solution.py:83
  296.7 0.6 dynamic_slice.27
  297.2 0.7 iota_compare_fusion.4
  297.9 0.2 reshape.166
  298.2 5.0 fusion.182
  303.2 1.9 fusion.183
  305.1 5.1 fusion.184
  310.1 0.2 copy.33
  310.3 0.3 broadcast_in_dim.117
  310.6 11.9 %constant_dynamic-slice_fusion.5 = (bf16[1,2048,1536]{1,2,0:T(8,128)(2,1)}, bf16[1,2048,1536]{1,2,0:T(8,128)(2,1)}) fusion(bf16[2,2048,1536]{1,2,0:T(8,128)(2,1)} %get-tuple-element.212, s32[]{:T(128)} %get-tuple-element.200, bf16[2,2048,1536]{1,2,0:T(8,128)(2,1)} %get-tuple-element.209), kind=kLoop, calls=%fused_computation.20.clone.1 | loop fusion | bytes 25165828 | tf_op jit(solution)/shard_map/while/body/jit(dynamic_index_in_dim)/dynamic_slice | solution.py:83
  322.6 0.6 dynamic_slice.27
  323.2 0.7 iota_compare_fusion.4
  323.9 0.2 reshape.166
  324.1 5.0 fusion.182
  329.1 1.9 fusion.183
  331.0 5.1 fusion.184
  336.1 0.2 copy.33
  336.3 0.3 broadcast_in_dim.117
  336.6 5.0 convolution_bitcast_fusion
  341.6 0.8 fusion.37
  342.4 10.5 %reshape_reshape.6 = f32[18432,128]{1,0:T(8,128)} reshape(f32[1536,1536]{1,0:T(8,128)} %convolution_bitcast_fusion) | data formatting | bytes 18874368 | tf_op jit(solution)/shard_map/reshape;reshape | solution.py:34
  353.0 48.0 %gather_fusion = f32[23592,128]{1,0:T(8,128)} fusion(f32[18432,128]{1,0:T(8,128)} %reshape_reshape.6, s32[24576]{0:T(1024)S(1)} %pad_clamp_fusion), kind=kCustom, calls=%fused_computation | custom fusion | bytes 24252576 | tf_op jit(solution)/shard_map/jit(_take)/gather | solution.py:35
  401.3 22.9 %select_reduce_fusion = f32[23592]{0:T(1024)} fusion(f32[23592,128]{1,0:T(8,128)} %gather_fusion, s32[23592]{0:T(1024)S(1)} %copy-done.2, pred[23592]{0:T(1024)(128)(4,1)S(1)} %copy-done.4), kind=kLoop, calls=%fused_computation.25 | loop fusion | flops 12055512 | bytes 12291432 | tf_op jit(solution)/shard_map/reduce_sum | solution.py:38
  424.3 1.4 collective-permute-start
  425.7 1.3 collective-permute-start.1
  427.0 235.6 %all-reduce.2.cloned.1.call-done = f32[23592]{0:T(1024)} async-done(((f32[23592]{0:T(1024)}), f32[23592]{0:T(1024)}) %all-reduce.2.cloned.1.call-update) | async-done | bytes 94384 | tf_op jit(solution)/shard_map/psum | solution.py:120
  662.5 1.5 broadcast_multiply_fusion
  664.1 1.2 fusion.85
  665.4 1.3 fusion.101
  666.9 0.8 fusion.100
  667.9 0.8 fusion.84
  668.7 0.3 stack.127
  669.1 1.2 gather_fusion.1
  670.3 0.3 select_reduce_fusion.1
  670.6 74.1 %psum.15 = f32[476]{0:T(512)S(1)} all-reduce(f32[476]{0:T(512)S(1)} %select_reduce_fusion.1), channel_id=1, replica_groups=mesh['dp'=8,'seq'=32] {'dp','seq'}, use_global_device_ids=true, to_apply=%region_38.39 | all-reduce | flops 476 | bytes 3808 | tf_op jit(solution)/shard_map/psum | solution.py:120
  744.7 0.6 broadcast_multiply_fusion.1
  745.6 4.5 fusion.70
  (197 shorter events, 0.7 us)
Async XLA Ops:
  7.2 127.1 %all-gather.3.cloned.1.call-start = ((), (), s32[]{:S(2)}) async-start(), calls=%async_computation | async-start | bytes 12976128 | tf_op jit(solution)/shard_map/all_gather | solution.py:63
  9.4 244.2 %all-gather.5.cloned.1.call-start = ((), (), s32[]{:S(2)}) async-start(), calls=%async_computation.1 | async-start | bytes 12976128 | tf_op jit(solution)/shard_map/all_gather | solution.py:62
  11.6 650.9 %all-reduce.2.cloned.1.call-start = ((), (), s32[]{:S(2)}) async-start(), calls=%async_computation.2 | async-start | bytes 196608 | tf_op jit(solution)/shard_map/psum | solution.py:120
  12.6 14.5 %collective-permute-start.2 = (bf16[2,15,1536]{2,1,0:T(8,128)(2,1)S(1)}, bf16[2,15,1536]{2,1,0:T(8,128)(2,1)S(1)}, u32[]{:S(2)}, u32[]{:S(2)}) collective-permute-start(bf16[2,15,1536]{2,1,0:T(8,128)(2,1)S(1)} %get-tuple-element.144), channel_id=1, source_target_pairs={{0,1},{1,2},{2,3},{3,4},{4,5},{5,6},{6,7},{7,8},{8,9},{9,10},{10,1... | collective-permute-start | bytes 276488 | tf_op jit(solution)/shard_map/ppermute | solution.py:18
  17.0 10.1 %collective-permute-start.3 = (bf16[2,15,1536]{2,1,0:T(8,128)(2,1)S(1)}, bf16[2,15,1536]{2,1,0:T(8,128)(2,1)S(1)}, u32[]{:S(2)}, u32[]{:S(2)}) collective-permute-start(bf16[2,15,1536]{2,1,0:T(8,128)(2,1)S(1)} %get-tuple-element.145), channel_id=1, source_target_pairs={{1,0},{2,1},{3,2},{4,3},{5,4},{6,5},{7,6},{8,7},{9,8},{10,9},{11,1... | collective-permute-start | bytes 276488 | tf_op jit(solution)/shard_map/ppermute | solution.py:19
  19.5 12.3 %copy-start.43 = (f32[1536]{0:T(1024)}, f32[1536]{0:T(1024)S(1)}, u32[]{:S(2)}) copy-start(f32[1536]{0:T(1024)S(1)} %get-tuple-element.112) | copy-start | bytes 18436
  19.5 12.3 %copy-start.45 = (f32[1536]{0:T(1024)}, f32[1536]{0:T(1024)S(1)}, u32[]{:S(2)}) copy-start(f32[1536]{0:T(1024)S(1)} %get-tuple-element.113) | copy-start | bytes 18436
  19.5 12.3 %copy-start.47 = (f32[1536]{0:T(1024)}, f32[1536]{0:T(1024)S(1)}, u32[]{:S(2)}) copy-start(f32[1536]{0:T(1024)S(1)} %get-tuple-element.114) | copy-start | bytes 18436
  19.5 12.3 %copy-start.49 = (f32[1536]{0:T(1024)}, f32[1536]{0:T(1024)S(1)}, u32[]{:S(2)}) copy-start(f32[1536]{0:T(1024)S(1)} %get-tuple-element.115) | copy-start | bytes 18436
  19.5 12.3 %copy-start.51 = (f32[1536]{0:T(1024)}, f32[1536]{0:T(1024)S(1)}, u32[]{:S(2)}) copy-start(f32[1536]{0:T(1024)S(1)} %get-tuple-element.116) | copy-start | bytes 18436
  19.5 12.3 %copy-start.53 = (f32[1536]{0:T(1024)}, f32[1536]{0:T(1024)S(1)}, u32[]{:S(2)}) copy-start(f32[1536]{0:T(1024)S(1)} %get-tuple-element.117) | copy-start | bytes 18436
  19.5 12.3 %copy-start.55 = (f32[1536]{0:T(1024)}, f32[1536]{0:T(1024)S(1)}, u32[]{:S(2)}) copy-start(f32[1536]{0:T(1024)S(1)} %get-tuple-element.118) | copy-start | bytes 18436
  19.5 12.3 %copy-start.57 = (f32[1536]{0:T(1024)}, f32[1536]{0:T(1024)S(1)}, u32[]{:S(2)}) copy-start(f32[1536]{0:T(1024)S(1)} %get-tuple-element.119) | copy-start | bytes 18436
  19.6 12.3 %copy-start.59 = (f32[1536]{0:T(1024)}, f32[1536]{0:T(1024)S(1)}, u32[]{:S(2)}) copy-start(f32[1536]{0:T(1024)S(1)} %get-tuple-element.120) | copy-start | bytes 18436
  19.6 12.3 %copy-start.61 = (f32[1536]{0:T(1024)}, f32[1536]{0:T(1024)S(1)}, u32[]{:S(2)}) copy-start(f32[1536]{0:T(1024)S(1)} %get-tuple-element.121) | copy-start | bytes 18436
  19.6 12.3 %copy-start.63 = (f32[1536]{0:T(1024)}, f32[1536]{0:T(1024)S(1)}, u32[]{:S(2)}) copy-start(f32[1536]{0:T(1024)S(1)} %get-tuple-element.122) | copy-start | bytes 18436
  19.6 12.3 %copy-start.65 = (f32[1536]{0:T(1024)}, f32[1536]{0:T(1024)S(1)}, u32[]{:S(2)}) copy-start(f32[1536]{0:T(1024)S(1)} %get-tuple-element.123) | copy-start | bytes 18436
  19.9 12.0 %copy-start.5 = (f32[1536]{0:T(1024)}, f32[1536]{0:T(1024)S(1)}, u32[]{:S(2)}) copy-start(f32[1536]{0:T(1024)S(1)} %get-tuple-element.93) | copy-start | bytes 18436
  19.9 12.0 %copy-start.7 = (f32[1536]{0:T(1024)}, f32[1536]{0:T(1024)S(1)}, u32[]{:S(2)}) copy-start(f32[1536]{0:T(1024)S(1)} %get-tuple-element.94) | copy-start | bytes 18436
  19.9 12.0 %copy-start.9 = (f32[1536]{0:T(1024)}, f32[1536]{0:T(1024)S(1)}, u32[]{:S(2)}) copy-start(f32[1536]{0:T(1024)S(1)} %get-tuple-element.95) | copy-start | bytes 18436
  19.9 12.0 %copy-start.11 = (f32[1536]{0:T(1024)}, f32[1536]{0:T(1024)S(1)}, u32[]{:S(2)}) copy-start(f32[1536]{0:T(1024)S(1)} %get-tuple-element.96) | copy-start | bytes 18436
  20.0 12.0 %copy-start.13 = (f32[1536]{0:T(1024)}, f32[1536]{0:T(1024)S(1)}, u32[]{:S(2)}) copy-start(f32[1536]{0:T(1024)S(1)} %get-tuple-element.97) | copy-start | bytes 18436
  20.0 12.0 %copy-start.15 = (f32[1536]{0:T(1024)}, f32[1536]{0:T(1024)S(1)}, u32[]{:S(2)}) copy-start(f32[1536]{0:T(1024)S(1)} %get-tuple-element.98) | copy-start | bytes 18436
  165.4 119.3 %copy-start.1 = (bf16[2,64,1536]{2,1,0:T(8,128)(2,1)S(1)}, bf16[2,64,1536]{2,1,0:T(8,128)(2,1)}, u32[]{:S(2)}) copy-start(bf16[2,64,1536]{2,1,0:T(8,128)(2,1)} %param.12) | copy-start | bytes 1179652
  165.4 119.3 %copy-start.70 = (s32[2]{0:T(128)S(1)}, s32[2]{0:T(128)}, u32[]{:S(2)}) copy-start(s32[2]{0:T(128)} %param.16) | copy-start | bytes 28
  353.0 48.0 %copy-start.2 = (s32[23592]{0:T(1024)S(1)}, s32[23592]{0:T(1024)}, u32[]{:S(2)}) copy-start(s32[23592]{0:T(1024)} %add_select_fusion.1) | copy-start | bytes 283108
  353.0 48.0 %copy-start.4 = (pred[23592]{0:T(1024)(128)(4,1)S(1)}, pred[23592]{0:T(1024)(128)(4,1)}, u32[]{:S(2)}) copy-start(pred[23592]{0:T(1024)(128)(4,1)} %get-tuple-element.138) | copy-start | bytes 70780
  400.9 263.2 %copy-start = (bf16[2,64,1536]{2,1,0:T(8,128)(2,1)S(1)}, bf16[2,64,1536]{2,1,0:T(8,128)(2,1)}, u32[]{:S(2)}) copy-start(bf16[2,64,1536]{2,1,0:T(8,128)(2,1)} %param.19) | copy-start | bytes 1179652
  400.9 268.2 %copy-start.67 = (s32[1024]{0:T(1024)S(1)}, s32[1024]{0:T(1024)}, u32[]{:S(2)}) copy-start(s32[1024]{0:T(1024)} %pad_clamp_fusion.1) | copy-start | bytes 12292
  401.0 269.3 %copy-start.68 = (s32[476]{0:T(512)S(1)}, s32[476]{0:T(512)}, u32[]{:S(2)}) copy-start(s32[476]{0:T(512)} %add_select_fusion.3) | copy-start | bytes 5716
  401.0 269.3 %copy-start.69 = (pred[476]{0:T(512)(128)(4,1)S(1)}, pred[476]{0:T(512)(128)(4,1)}, u32[]{:S(2)}) copy-start(pred[476]{0:T(512)(128)(4,1)} %get-tuple-element.136) | copy-start | bytes 1432
  401.0 344.3 %copy-start.6 = (f32[1536]{0:T(1024)S(1)}, f32[1536]{0:T(1024)}, u32[]{:S(2)}) copy-start(f32[1536]{0:T(1024)} %copy-done.5) | copy-start | bytes 18436
  401.0 344.3 %copy-start.8 = (f32[1536]{0:T(1024)S(1)}, f32[1536]{0:T(1024)}, u32[]{:S(2)}) copy-start(f32[1536]{0:T(1024)} %copy-done.7) | copy-start | bytes 18436
  401.0 344.3 %copy-start.10 = (f32[1536]{0:T(1024)S(1)}, f32[1536]{0:T(1024)}, u32[]{:S(2)}) copy-start(f32[1536]{0:T(1024)} %copy-done.9) | copy-start | bytes 18436
  401.0 344.3 %copy-start.12 = (f32[1536]{0:T(1024)S(1)}, f32[1536]{0:T(1024)}, u32[]{:S(2)}) copy-start(f32[1536]{0:T(1024)} %copy-done.11) | copy-start | bytes 18436
  401.0 344.3 %copy-start.14 = (f32[1536]{0:T(1024)S(1)}, f32[1536]{0:T(1024)}, u32[]{:S(2)}) copy-start(f32[1536]{0:T(1024)} %copy-done.13) | copy-start | bytes 18436
  401.0 344.3 %copy-start.16 = (f32[1536]{0:T(1024)S(1)}, f32[1536]{0:T(1024)}, u32[]{:S(2)}) copy-start(f32[1536]{0:T(1024)} %copy-done.15) | copy-start | bytes 18436
  401.0 344.3 %copy-start.18 = (f32[1536]{0:T(1024)S(1)}, f32[1536]{0:T(1024)}, u32[]{:S(2)}) copy-start(f32[1536]{0:T(1024)} %copy-done.17) | copy-start | bytes 18436
  401.0 344.3 %copy-start.20 = (f32[1536]{0:T(1024)S(1)}, f32[1536]{0:T(1024)}, u32[]{:S(2)}) copy-start(f32[1536]{0:T(1024)} %copy-done.19) | copy-start | bytes 18436
  401.1 344.3 %copy-start.22 = (f32[1536]{0:T(1024)S(1)}, f32[1536]{0:T(1024)}, u32[]{:S(2)}) copy-start(f32[1536]{0:T(1024)} %copy-done.21) | copy-start | bytes 18436
  401.1 344.3 %copy-start.24 = (f32[1536]{0:T(1024)S(1)}, f32[1536]{0:T(1024)}, u32[]{:S(2)}) copy-start(f32[1536]{0:T(1024)} %copy-done.23) | copy-start | bytes 18436
  401.1 344.3 %copy-start.26 = (f32[1536]{0:T(1024)S(1)}, f32[1536]{0:T(1024)}, u32[]{:S(2)}) copy-start(f32[1536]{0:T(1024)} %copy-done.25) | copy-start | bytes 18436
  401.1 344.3 %copy-start.28 = (f32[1536]{0:T(1024)S(1)}, f32[1536]{0:T(1024)}, u32[]{:S(2)}) copy-start(f32[1536]{0:T(1024)} %copy-done.27) | copy-start | bytes 18436
  401.1 344.3 %copy-start.30 = (f32[1536]{0:T(1024)S(1)}, f32[1536]{0:T(1024)}, u32[]{:S(2)}) copy-start(f32[1536]{0:T(1024)} %copy-done.29) | copy-start | bytes 18436
  401.1 344.3 %copy-start.32 = (f32[1536]{0:T(1024)S(1)}, f32[1536]{0:T(1024)}, u32[]{:S(2)}) copy-start(f32[1536]{0:T(1024)} %copy-done.31) | copy-start | bytes 18436
  401.1 344.3 %copy-start.34 = (f32[1536]{0:T(1024)S(1)}, f32[1536]{0:T(1024)}, u32[]{:S(2)}) copy-start(f32[1536]{0:T(1024)} %copy-done.33) | copy-start | bytes 18436
  401.1 344.3 %copy-start.36 = (f32[1536]{0:T(1024)S(1)}, f32[1536]{0:T(1024)}, u32[]{:S(2)}) copy-start(f32[1536]{0:T(1024)} %copy-done.35) | copy-start | bytes 18436
  401.1 344.3 %copy-start.38 = (f32[1536]{0:T(1024)S(1)}, f32[1536]{0:T(1024)}, u32[]{:S(2)}) copy-start(f32[1536]{0:T(1024)} %copy-done.37) | copy-start | bytes 18436
  401.1 344.3 %copy-start.40 = (f32[1536]{0:T(1024)S(1)}, f32[1536]{0:T(1024)}, u32[]{:S(2)}) copy-start(f32[1536]{0:T(1024)} %copy-done.39) | copy-start | bytes 18436
  401.2 344.3 %copy-start.42 = (f32[1536]{0:T(1024)S(1)}, f32[1536]{0:T(1024)}, u32[]{:S(2)}) copy-start(f32[1536]{0:T(1024)} %copy-done.41) | copy-start | bytes 18436
  401.2 344.3 %copy-start.44 = (f32[1536]{0:T(1024)S(1)}, f32[1536]{0:T(1024)}, u32[]{:S(2)}) copy-start(f32[1536]{0:T(1024)} %copy-done.43) | copy-start | bytes 18436
  401.2 344.3 %copy-start.46 = (f32[1536]{0:T(1024)S(1)}, f32[1536]{0:T(1024)}, u32[]{:S(2)}) copy-start(f32[1536]{0:T(1024)} %copy-done.45) | copy-start | bytes 18436
  401.2 344.3 %copy-start.48 = (f32[1536]{0:T(1024)S(1)}, f32[1536]{0:T(1024)}, u32[]{:S(2)}) copy-start(f32[1536]{0:T(1024)} %copy-done.47) | copy-start | bytes 18436
  401.2 344.3 %copy-start.50 = (f32[1536]{0:T(1024)S(1)}, f32[1536]{0:T(1024)}, u32[]{:S(2)}) copy-start(f32[1536]{0:T(1024)} %copy-done.49) | copy-start | bytes 18436
  401.2 344.3 %copy-start.52 = (f32[1536]{0:T(1024)S(1)}, f32[1536]{0:T(1024)}, u32[]{:S(2)}) copy-start(f32[1536]{0:T(1024)} %copy-done.51) | copy-start | bytes 18436
  401.2 344.3 %copy-start.54 = (f32[1536]{0:T(1024)S(1)}, f32[1536]{0:T(1024)}, u32[]{:S(2)}) copy-start(f32[1536]{0:T(1024)} %copy-done.53) | copy-start | bytes 18436
  401.2 344.3 %copy-start.56 = (f32[1536]{0:T(1024)S(1)}, f32[1536]{0:T(1024)}, u32[]{:S(2)}) copy-start(f32[1536]{0:T(1024)} %copy-done.55) | copy-start | bytes 18436
  401.2 344.3 %copy-start.58 = (f32[1536]{0:T(1024)S(1)}, f32[1536]{0:T(1024)}, u32[]{:S(2)}) copy-start(f32[1536]{0:T(1024)} %copy-done.57) | copy-start | bytes 18436
  401.2 344.3 %copy-start.60 = (f32[1536]{0:T(1024)S(1)}, f32[1536]{0:T(1024)}, u32[]{:S(2)}) copy-start(f32[1536]{0:T(1024)} %copy-done.59) | copy-start | bytes 18436
  401.3 344.3 %copy-start.62 = (f32[1536]{0:T(1024)S(1)}, f32[1536]{0:T(1024)}, u32[]{:S(2)}) copy-start(f32[1536]{0:T(1024)} %copy-done.61) | copy-start | bytes 18436
  401.3 344.3 %copy-start.64 = (f32[1536]{0:T(1024)S(1)}, f32[1536]{0:T(1024)}, u32[]{:S(2)}) copy-start(f32[1536]{0:T(1024)} %copy-done.63) | copy-start | bytes 18436
  401.3 344.3 %copy-start.66 = (f32[1536]{0:T(1024)S(1)}, f32[1536]{0:T(1024)}, u32[]{:S(2)}) copy-start(f32[1536]{0:T(1024)} %copy-done.65) | copy-start | bytes 18436
  424.3 239.8 %collective-permute-start = (bf16[2,15,1536]{2,1,0:T(8,128)(2,1)S(1)}, bf16[2,15,1536]{2,1,0:T(8,128)(2,1)S(1)}, u32[]{:S(2)}, u32[]{:S(2)}) collective-permute-start(bf16[2,15,1536]{2,1,0:T(8,128)(2,1)S(1)} %get-tuple-element.146), channel_id=1, source_target_pairs={{0,1},{1,2},{2,3},{3,4},{4,5},{5,6},{6,7},{7,8},{8,9},{9,10},{10,1... | collective-permute-start | bytes 276488 | tf_op jit(solution)/shard_map/ppermute | solution.py:18
  425.7 239.7 %collective-permute-start.1 = (bf16[2,15,1536]{2,1,0:T(8,128)(2,1)S(1)}, bf16[2,15,1536]{2,1,0:T(8,128)(2,1)S(1)}, u32[]{:S(2)}, u32[]{:S(2)}) collective-permute-start(bf16[2,15,1536]{2,1,0:T(8,128)(2,1)S(1)} %get-tuple-element.147), channel_id=1, source_target_pairs={{1,0},{2,1},{3,2},{4,3},{5,4},{6,5},{7,6},{8,7},{9,8},{10,9},{11,1... | collective-permute-start | bytes 276488 | tf_op jit(solution)/shard_map/ppermute | solution.py:19
  (18 other events, 180.0 us)
Sparse Core Ops, SparseCore 0:
  11.2 123.0 all-gather.2
  136.8 116.7 all-gather.4
  424.3 238.1 all-reduce.1
where the time goes:
time: 759 us; the launch traced here: 757 us
  waiting for transfers between devices  424 us (56%)
  local copies, waits for them, and re-layouts  155 us (20%)
  blocking collectives  74.1 us (10%)
  other arithmetic  51.7 us (7%)
  matrix products  28.4 us (4%)
  between operations  15.2 us (2%)
  starting transfers between devices  8.5 us (1%)
    psum x1, waiting for transfers between devices, on_device(): weight_sum, kernel_sum = lax.psum((weight_vals, kernel_vals), ('dp', 'seq'))  236 us
    all_gather x1, waiting for transfers between devices, on_device(): lax.all_gather(value_rows, 'seq', axis=1, tiled=True)  99.7 us
    all_gather x1, waiting for transfers between devices, on_device(): lax.all_gather(key_rows, 'seq', axis=1, tiled=True)  88.2 us
    psum x1, blocking collectives, on_device(): weight_sum, kernel_sum = lax.psum((weight_vals, kernel_vals), ('dp', 'seq'))  74.1 us
    unnamed x154, local copies, waits for them, and re-layouts  66.9 us
    gather x2, local copies, waits for them, and re-layouts, pick_entries(): chosen = jnp.take(blocks, picks // lane, axis=0)  49.1 us
    dynamic_slice x6, local copies, waits for them, and re-layouts, on_device(): context = lax.map(one_utt, (queries, all_keys, all_values, utt_lengths))  25.1 us
    reduce_sum x2, other arithmetic, pick_entries(): return jnp.sum(jnp.where(hit, chosen, jnp.float32(0.0)), axis=1)  23.2 us
  transfers between devices with their start and end apart: 7, of which 3 were waited for; matrix products, arithmetic and copies ran while one was open for 7% of the time, Pallas kernels for 0%

commit v1 on v0

--- a/solution.py
+++ b/solution.py
@@ -117,7 +117,9 @@
     context_grad = context_grad.reshape(local_utts, frames_dev, width).astype(jnp.bfloat16)
     weight_vals = pick_entries(weight_grad, pick_weight)
     kernel_vals = pick_entries(kernel_grad, pick_kernel)
-    weight_sum, kernel_sum = lax.psum((weight_vals, kernel_vals), ("dp", "seq"))
+    weight_sum, kernel_sum = lax.psum(
+        lax.psum((weight_vals, kernel_vals), axis_name="dp"), axis_name="seq"
+    )
     total_slots = local_utts * lax.axis_size("dp") * full_frames
     norm_factor = 1.0 / math.sqrt(total_slots)
     return (conv_out, context_grad, weight_sum * norm_factor, kernel_sum * norm_factor)

time: 759 us -> 644 us (0.85)
  waiting for transfers between devices: 424 us -> 299 us
    psum x1 -> x2, waiting for transfers between devices: 236 us -> 107 us  [the longest x1 54.1 us: on_device(): lax.psum((weight_vals, kernel_vals), axis_name='dp')]
    psum x1 -> x2, blocking collectives: 74.1 us -> 75.5 us  [the longest x1 61 us: on_device(): lax.psum(lax.psum((weight_vals, kernel_vals), axis_name='dp'), axis_name=...]
    unnamed x154 -> x146, local copies, waits for them, and re-layouts: 66.9 us -> 66.8 us
  transfers between devices with their start and end apart: 7 -> 8, of which waited for: 3 -> 4; matrix products, arithmetic and copies ran while one was open for 7% -> 23% of each run, Pallas kernels for 0% -> 0%
where the time goes in v1:
time: 644 us; the launch traced here: 638 us
  waiting for transfers between devices  299 us (46%)
  local copies, waits for them, and re-layouts  155 us (24%)
  blocking collectives  75.5 us (12%)
  other arithmetic  51.3 us (8%)
  matrix products  33.1 us (5%)
  between operations  15.2 us (2%)
  starting transfers between devices  8.72 us (1%)
    all_gather x1, waiting for transfers between devices, on_device(): lax.all_gather(value_rows, 'seq', axis=1, tiled=True)  102 us
    all_gather x1, waiting for transfers between devices, on_device(): lax.all_gather(key_rows, 'seq', axis=1, tiled=True)  88.8 us
    unnamed x146, local copies, waits for them, and re-layouts  66.8 us
    psum x1, blocking collectives, on_device(): lax.psum(lax.psum((weight_vals, kernel_vals), axis_name='dp'), axis_name=...  61 us
    psum x1, waiting for transfers between devices, on_device(): lax.psum((weight_vals, kernel_vals), axis_name='dp')  54.1 us
    psum x1, waiting for transfers between devices, on_device(): lax.psum(lax.psum((weight_vals, kernel_vals), axis_name='dp'), axis_name=...  53.3 us
    gather x2, local copies, waits for them, and re-layouts, pick_entries(): chosen = jnp.take(blocks, picks // lane, axis=0)  49.1 us
    dynamic_slice x6, local copies, waits for them, and re-layouts, on_device(): context = lax.map(one_utt, (queries, all_keys, all_values, utt_lengths))  25.1 us
  transfers between devices with their start and end apart: 8, of which 4 were waited for; matrix products, arithmetic and copies ran while one was open for 23% of the time, Pallas kernels for 0%

profile of v1, /device:TPU:1, one launch (start us, length us, event | category | flops | bytes accessed | tf_op | source)
XLA Modules:
  0.0 637.8 jit_solution(4167659140105766210)
XLA Ops:
  7.2 2.1 copy.22
  9.4 0.0 all-gather.5.cloned.1.call-start
  9.4 2.1 copy.23
  11.6 0.0 all-reduce.3.cloned.1.call-start
  11.7 1.0 fusion.165
  12.6 4.4 collective-permute-start.2
  17.0 1.3 collective-permute-start.3
  18.3 0.9 convert_element_type.130
  19.3 0.2 slice_reduce_fusion.29
  19.6 0.3 slice_reduce_fusion.30
  20.1 0.7 compare_convert_fusion
  20.8 1.3 add_select_fusion.3
  22.1 1.3 compare_and_fusion.1
  23.3 1.6 compare_and_fusion
  24.9 1.6 add_select_fusion.1
  26.5 0.6 pad_clamp_fusion.1
  27.1 1.2 maximum_convert_fusion
  28.3 3.1 fusion.104
  31.8 102.5 %all-gather.3.cloned.1.call-done = bf16[2,2048,1536]{2,0,1:T(2,128)(2,1)} async-done(((bf16[2,64,1536]{2,0,1:T(2,128)(2,1)}), bf16[2,2048,1536]{2,0,1:T(2,128)(2,1)}) %all-gather.3.cloned.1.call-update) | async-done | bytes 12582928 | tf_op jit(solution)/shard_map/all_gather | solution.py:63
  134.2 31.1 %copy.24 = bf16[2,2048,1536]{1,2,0:T(8,128)(2,1)} copy(bf16[2,2048,1536]{2,0,1:T(2,128)(2,1)} %all-gather.3.cloned.1.call-done) | data formatting | bytes 25165824
  165.3 88.8 %all-gather.5.cloned.1.call-done = bf16[2,2048,1536]{2,0,1:T(2,128)(2,1)} async-done(((bf16[2,64,1536]{2,0,1:T(2,128)(2,1)}), bf16[2,2048,1536]{2,0,1:T(2,128)(2,1)}) %all-gather.5.cloned.1.call-update) | async-done | bytes 12582928 | tf_op jit(solution)/shard_map/all_gather | solution.py:62
  254.2 31.1 %copy.25 = bf16[2,2048,1536]{1,2,0:T(8,128)(2,1)} copy(bf16[2,2048,1536]{2,0,1:T(2,128)(2,1)} %all-gather.5.cloned.1.call-done) | data formatting | bytes 25165824
  285.3 51.9 %while.11 = (s32[]{:T(128)}, bf16[2,64,1536]{2,1,0:T(8,128)(2,1)S(1)}, bf16[2,2048,1536]{1,2,0:T(8,128)(2,1)}, s32[2]{0:T(128)S(1)}, bf16[2,64,1536]{2,1,0:T(8,1...) while((s32[]{:T(128)}, bf16[2,64,1536]{2,1,0:T(8,128)(2,1)S(1)}, ...), condition=%wide.region_3.4_spmd.clone, body=%wide.region_0.3_spmd.clone.sunk | while | flops 828571648 | bytes 65302632 | solution.py:83
  285.3 12.0 %constant_dynamic-slice_fusion.5 = (bf16[1,2048,1536]{1,2,0:T(8,128)(2,1)}, bf16[1,2048,1536]{1,2,0:T(8,128)(2,1)}) fusion(bf16[2,2048,1536]{1,2,0:T(8,128)(2,1)} %get-tuple-element.212, s32[]{:T(128)} %get-tuple-element.200, bf16[2,2048,1536]{1,2,0:T(8,128)(2,1)} %get-tuple-element.209), kind=kLoop, calls=%fused_computation.20.clone.1 | loop fusion | bytes 25165828 | tf_op jit(solution)/shard_map/while/body/jit(dynamic_index_in_dim)/dynamic_slice | solution.py:83
  297.3 0.6 dynamic_slice.27
  297.9 0.7 iota_compare_fusion.4
  298.6 0.2 reshape.166
  298.8 5.0 fusion.182
  303.8 1.9 fusion.183
  305.7 5.1 fusion.184
  310.8 0.2 copy.33
  311.0 0.3 broadcast_in_dim.117
  311.3 11.9 %constant_dynamic-slice_fusion.5 = (bf16[1,2048,1536]{1,2,0:T(8,128)(2,1)}, bf16[1,2048,1536]{1,2,0:T(8,128)(2,1)}) fusion(bf16[2,2048,1536]{1,2,0:T(8,128)(2,1)} %get-tuple-element.212, s32[]{:T(128)} %get-tuple-element.200, bf16[2,2048,1536]{1,2,0:T(8,128)(2,1)} %get-tuple-element.209), kind=kLoop, calls=%fused_computation.20.clone.1 | loop fusion | bytes 25165828 | tf_op jit(solution)/shard_map/while/body/jit(dynamic_index_in_dim)/dynamic_slice | solution.py:83
  323.2 0.6 dynamic_slice.27
  323.8 0.7 iota_compare_fusion.4
  324.5 0.2 reshape.166
  324.7 5.0 fusion.182
  329.7 1.9 fusion.183
  331.6 5.1 fusion.184
  336.7 0.2 copy.33
  336.9 0.3 broadcast_in_dim.117
  337.2 3.2 fusion.37
  340.4 1.6 collective-permute-start
  342.0 5.0 convolution_bitcast_fusion
  347.1 10.5 %reshape_reshape.6 = f32[18432,128]{1,0:T(8,128)} reshape(f32[1536,1536]{1,0:T(8,128)} %convolution_bitcast_fusion) | data formatting | bytes 18874368 | tf_op jit(solution)/shard_map/reshape;reshape | solution.py:34
  357.6 48.0 %gather_fusion = f32[23592,128]{1,0:T(8,128)} fusion(f32[18432,128]{1,0:T(8,128)} %reshape_reshape.6, s32[24576]{0:T(1024)S(1)} %pad_clamp_fusion), kind=kCustom, calls=%fused_computation | custom fusion | bytes 24252576 | tf_op jit(solution)/shard_map/jit(_take)/gather | solution.py:35
  405.5 22.9 %select_reduce_fusion = f32[23592]{0:T(1024)} fusion(f32[23592,128]{1,0:T(8,128)} %gather_fusion, s32[23592]{0:T(1024)S(1)} %copy-done.2, pred[23592]{0:T(1024)(128)(4,1)S(1)} %copy-done.4), kind=kLoop, calls=%fused_computation.25 | loop fusion | flops 12055512 | bytes 12291432 | tf_op jit(solution)/shard_map/reduce_sum | solution.py:38
  428.8 0.0 all-reduce.5.cloned.1.call-start
  428.8 4.7 fusion.34
  433.5 1.3 collective-permute-start.1
  434.8 54.1 %all-reduce.3.cloned.1.call-done = f32[23592]{0:T(1024)} async-done(((f32[23592]{0:T(1024)}), f32[23592]{0:T(1024)}) %all-reduce.3.cloned.1.call-update) | async-done | bytes 94384 | tf_op jit(solution)/shard_map/psum | solution.py:121
  489.0 1.2 fusion.85
  490.3 1.3 fusion.101
  491.8 0.8 fusion.100
  492.7 0.8 fusion.84
  493.6 0.3 stack.127
  494.0 1.2 gather_fusion.1
  495.2 0.3 select_reduce_fusion.1
  495.5 14.5 %psum.30 = f32[476]{0:T(512)S(1)} all-reduce(f32[476]{0:T(512)S(1)} %select_reduce_fusion.1), channel_id=1, replica_groups=mesh['dp'=8,'seq'=32] {'dp'}, use_global_device_ids=true, to_apply=%region_39.40 | all-reduce | flops 476 | bytes 3808 | tf_op jit(solution)/shard_map/psum | solution.py:121
  510.0 61.0 %psum.31 = f32[476]{0:T(512)S(1)} all-reduce(f32[476]{0:T(512)S(1)} %psum.30), channel_id=1, replica_groups=mesh['dp'=8,'seq'=32] {'seq'}, use_global_device_ids=true, to_apply=%region_40.41 | all-reduce | flops 476 | bytes 3808 | tf_op jit(solution)/shard_map/psum | solution.py:120
  571.3 4.5 fusion.70
  575.8 0.6 broadcast_multiply_fusion.1
  576.4 53.3 %all-reduce.5.cloned.1.call-done = f32[23592]{0:T(1024)} async-done(((f32[23592]{0:T(1024)}), f32[23592]{0:T(1024)}) %all-reduce.5.cloned.1.call-update) | async-done | bytes 94384 | tf_op jit(solution)/shard_map/psum | solution.py:120
  629.7 1.5 broadcast_multiply_fusion
  (191 shorter events, 0.8 us)
Async XLA Ops:
  7.2 127.1 %all-gather.3.cloned.1.call-start = ((), (), s32[]{:S(2)}) async-start(), calls=%async_computation | async-start | bytes 12976128 | tf_op jit(solution)/shard_map/all_gather | solution.py:63
  9.4 244.8 %all-gather.5.cloned.1.call-start = ((), (), s32[]{:S(2)}) async-start(), calls=%async_computation.1 | async-start | bytes 12976128 | tf_op jit(solution)/shard_map/all_gather | solution.py:62
  11.6 477.3 %all-reduce.3.cloned.1.call-start = ((), (), s32[]{:S(2)}) async-start(), calls=%async_computation.2 | async-start | bytes 196608 | tf_op jit(solution)/shard_map/psum | solution.py:121
  12.6 14.5 %collective-permute-start.2 = (bf16[2,15,1536]{2,1,0:T(8,128)(2,1)S(1)}, bf16[2,15,1536]{2,1,0:T(8,128)(2,1)S(1)}, u32[]{:S(2)}, u32[]{:S(2)}) collective-permute-start(bf16[2,15,1536]{2,1,0:T(8,128)(2,1)S(1)} %get-tuple-element.144), channel_id=1, source_target_pairs={{0,1},{1,2},{2,3},{3,4},{4,5},{5,6},{6,7},{7,8},{8,9},{9,10},{10,1... | collective-permute-start | bytes 276488 | tf_op jit(solution)/shard_map/ppermute | solution.py:18
  17.0 10.1 %collective-permute-start.3 = (bf16[2,15,1536]{2,1,0:T(8,128)(2,1)S(1)}, bf16[2,15,1536]{2,1,0:T(8,128)(2,1)S(1)}, u32[]{:S(2)}, u32[]{:S(2)}) collective-permute-start(bf16[2,15,1536]{2,1,0:T(8,128)(2,1)S(1)} %get-tuple-element.145), channel_id=1, source_target_pairs={{1,0},{2,1},{3,2},{4,3},{5,4},{6,5},{7,6},{8,7},{9,8},{10,9},{11,1... | collective-permute-start | bytes 276488 | tf_op jit(solution)/shard_map/ppermute | solution.py:19
  19.5 12.0 %copy-start.43 = (f32[1536]{0:T(1024)}, f32[1536]{0:T(1024)S(1)}, u32[]{:S(2)}) copy-start(f32[1536]{0:T(1024)S(1)} %get-tuple-element.112) | copy-start | bytes 18436
  19.5 12.0 %copy-start.45 = (f32[1536]{0:T(1024)}, f32[1536]{0:T(1024)S(1)}, u32[]{:S(2)}) copy-start(f32[1536]{0:T(1024)S(1)} %get-tuple-element.113) | copy-start | bytes 18436
  19.5 12.0 %copy-start.47 = (f32[1536]{0:T(1024)}, f32[1536]{0:T(1024)S(1)}, u32[]{:S(2)}) copy-start(f32[1536]{0:T(1024)S(1)} %get-tuple-element.114) | copy-start | bytes 18436
  19.5 12.0 %copy-start.49 = (f32[1536]{0:T(1024)}, f32[1536]{0:T(1024)S(1)}, u32[]{:S(2)}) copy-start(f32[1536]{0:T(1024)S(1)} %get-tuple-element.115) | copy-start | bytes 18436
  19.5 12.0 %copy-start.51 = (f32[1536]{0:T(1024)}, f32[1536]{0:T(1024)S(1)}, u32[]{:S(2)}) copy-start(f32[1536]{0:T(1024)S(1)} %get-tuple-element.116) | copy-start | bytes 18436
  19.5 12.0 %copy-start.53 = (f32[1536]{0:T(1024)}, f32[1536]{0:T(1024)S(1)}, u32[]{:S(2)}) copy-start(f32[1536]{0:T(1024)S(1)} %get-tuple-element.117) | copy-start | bytes 18436
  19.5 12.0 %copy-start.55 = (f32[1536]{0:T(1024)}, f32[1536]{0:T(1024)S(1)}, u32[]{:S(2)}) copy-start(f32[1536]{0:T(1024)S(1)} %get-tuple-element.118) | copy-start | bytes 18436
  19.5 12.0 %copy-start.57 = (f32[1536]{0:T(1024)}, f32[1536]{0:T(1024)S(1)}, u32[]{:S(2)}) copy-start(f32[1536]{0:T(1024)S(1)} %get-tuple-element.119) | copy-start | bytes 18436
  19.5 12.0 %copy-start.59 = (f32[1536]{0:T(1024)}, f32[1536]{0:T(1024)S(1)}, u32[]{:S(2)}) copy-start(f32[1536]{0:T(1024)S(1)} %get-tuple-element.120) | copy-start | bytes 18436
  19.6 12.0 %copy-start.61 = (f32[1536]{0:T(1024)}, f32[1536]{0:T(1024)S(1)}, u32[]{:S(2)}) copy-start(f32[1536]{0:T(1024)S(1)} %get-tuple-element.121) | copy-start | bytes 18436
  19.6 12.0 %copy-start.63 = (f32[1536]{0:T(1024)}, f32[1536]{0:T(1024)S(1)}, u32[]{:S(2)}) copy-start(f32[1536]{0:T(1024)S(1)} %get-tuple-element.122) | copy-start | bytes 18436
  19.6 12.0 %copy-start.65 = (f32[1536]{0:T(1024)}, f32[1536]{0:T(1024)S(1)}, u32[]{:S(2)}) copy-start(f32[1536]{0:T(1024)S(1)} %get-tuple-element.123) | copy-start | bytes 18436
  19.9 11.7 %copy-start.5 = (f32[1536]{0:T(1024)}, f32[1536]{0:T(1024)S(1)}, u32[]{:S(2)}) copy-start(f32[1536]{0:T(1024)S(1)} %get-tuple-element.93) | copy-start | bytes 18436
  19.9 11.7 %copy-start.7 = (f32[1536]{0:T(1024)}, f32[1536]{0:T(1024)S(1)}, u32[]{:S(2)}) copy-start(f32[1536]{0:T(1024)S(1)} %get-tuple-element.94) | copy-start | bytes 18436
  19.9 11.7 %copy-start.9 = (f32[1536]{0:T(1024)}, f32[1536]{0:T(1024)S(1)}, u32[]{:S(2)}) copy-start(f32[1536]{0:T(1024)S(1)} %get-tuple-element.95) | copy-start | bytes 18436
  19.9 11.7 %copy-start.11 = (f32[1536]{0:T(1024)}, f32[1536]{0:T(1024)S(1)}, u32[]{:S(2)}) copy-start(f32[1536]{0:T(1024)S(1)} %get-tuple-element.96) | copy-start | bytes 18436
  165.3 120.0 %copy-start.1 = (bf16[2,64,1536]{2,1,0:T(8,128)(2,1)S(1)}, bf16[2,64,1536]{2,1,0:T(8,128)(2,1)}, u32[]{:S(2)}) copy-start(bf16[2,64,1536]{2,1,0:T(8,128)(2,1)} %param.12) | copy-start | bytes 1179652
  165.3 120.0 %copy-start.70 = (s32[2]{0:T(128)S(1)}, s32[2]{0:T(128)}, u32[]{:S(2)}) copy-start(s32[2]{0:T(128)} %param.16) | copy-start | bytes 28
  285.3 51.9 %copy-start.3 = (bf16[2,64,1536]{2,1,0:T(8,128)(2,1)S(1)}, bf16[2,64,1536]{2,1,0:T(8,128)(2,1)}, u32[]{:S(2)}) copy-start(bf16[2,64,1536]{2,1,0:T(8,128)(2,1)} %param.15) | copy-start | bytes 1179652
  340.4 148.5 %collective-permute-start = (bf16[2,15,1536]{2,1,0:T(8,128)(2,1)S(1)}, bf16[2,15,1536]{2,1,0:T(8,128)(2,1)S(1)}, u32[]{:S(2)}, u32[]{:S(2)}) collective-permute-start(bf16[2,15,1536]{2,1,0:T(8,128)(2,1)S(1)} %get-tuple-element.146), channel_id=1, source_target_pairs={{0,1},{1,2},{2,3},{3,4},{4,5},{5,6},{6,7},{7,8},{8,9},{9,10},{10,1... | collective-permute-start | bytes 276488 | tf_op jit(solution)/shard_map/ppermute | solution.py:18
  357.6 48.0 %copy-start.2 = (s32[23592]{0:T(1024)S(1)}, s32[23592]{0:T(1024)}, u32[]{:S(2)}) copy-start(s32[23592]{0:T(1024)} %add_select_fusion.1) | copy-start | bytes 283108
  357.6 48.0 %copy-start.4 = (pred[23592]{0:T(1024)(128)(4,1)S(1)}, pred[23592]{0:T(1024)(128)(4,1)}, u32[]{:S(2)}) copy-start(pred[23592]{0:T(1024)(128)(4,1)} %get-tuple-element.138) | copy-start | bytes 70780
  405.5 83.4 %copy-start = (bf16[2,64,1536]{2,1,0:T(8,128)(2,1)S(1)}, bf16[2,64,1536]{2,1,0:T(8,128)(2,1)}, u32[]{:S(2)}) copy-start(bf16[2,64,1536]{2,1,0:T(8,128)(2,1)} %param.19) | copy-start | bytes 1179652
  428.4 65.5 %copy-start.67 = (s32[1024]{0:T(1024)S(1)}, s32[1024]{0:T(1024)}, u32[]{:S(2)}) copy-start(s32[1024]{0:T(1024)} %pad_clamp_fusion.1) | copy-start | bytes 12292
  428.4 66.7 %copy-start.68 = (s32[476]{0:T(512)S(1)}, s32[476]{0:T(512)}, u32[]{:S(2)}) copy-start(s32[476]{0:T(512)} %add_select_fusion.3) | copy-start | bytes 5716
  428.4 66.7 %copy-start.69 = (pred[476]{0:T(512)(128)(4,1)S(1)}, pred[476]{0:T(512)(128)(4,1)}, u32[]{:S(2)}) copy-start(pred[476]{0:T(512)(128)(4,1)} %get-tuple-element.136) | copy-start | bytes 1432
  428.4 142.6 %copy-start.6 = (f32[1536]{0:T(1024)S(1)}, f32[1536]{0:T(1024)}, u32[]{:S(2)}) copy-start(f32[1536]{0:T(1024)} %copy-done.5) | copy-start | bytes 18436
  428.4 142.6 %copy-start.8 = (f32[1536]{0:T(1024)S(1)}, f32[1536]{0:T(1024)}, u32[]{:S(2)}) copy-start(f32[1536]{0:T(1024)} %copy-done.7) | copy-start | bytes 18436
  428.5 142.6 %copy-start.10 = (f32[1536]{0:T(1024)S(1)}, f32[1536]{0:T(1024)}, u32[]{:S(2)}) copy-start(f32[1536]{0:T(1024)} %copy-done.9) | copy-start | bytes 18436
  428.5 142.6 %copy-start.12 = (f32[1536]{0:T(1024)S(1)}, f32[1536]{0:T(1024)}, u32[]{:S(2)}) copy-start(f32[1536]{0:T(1024)} %copy-done.11) | copy-start | bytes 18436
  428.5 142.6 %copy-start.14 = (f32[1536]{0:T(1024)S(1)}, f32[1536]{0:T(1024)}, u32[]{:S(2)}) copy-start(f32[1536]{0:T(1024)} %copy-done.13) | copy-start | bytes 18436
  428.5 142.6 %copy-start.16 = (f32[1536]{0:T(1024)S(1)}, f32[1536]{0:T(1024)}, u32[]{:S(2)}) copy-start(f32[1536]{0:T(1024)} %copy-done.15) | copy-start | bytes 18436
  428.5 142.6 %copy-start.18 = (f32[1536]{0:T(1024)S(1)}, f32[1536]{0:T(1024)}, u32[]{:S(2)}) copy-start(f32[1536]{0:T(1024)} %copy-done.17) | copy-start | bytes 18436
  428.5 142.6 %copy-start.20 = (f32[1536]{0:T(1024)S(1)}, f32[1536]{0:T(1024)}, u32[]{:S(2)}) copy-start(f32[1536]{0:T(1024)} %copy-done.19) | copy-start | bytes 18436
  428.5 142.6 %copy-start.22 = (f32[1536]{0:T(1024)S(1)}, f32[1536]{0:T(1024)}, u32[]{:S(2)}) copy-start(f32[1536]{0:T(1024)} %copy-done.21) | copy-start | bytes 18436
  428.5 142.6 %copy-start.24 = (f32[1536]{0:T(1024)S(1)}, f32[1536]{0:T(1024)}, u32[]{:S(2)}) copy-start(f32[1536]{0:T(1024)} %copy-done.23) | copy-start | bytes 18436
  428.5 142.6 %copy-start.26 = (f32[1536]{0:T(1024)S(1)}, f32[1536]{0:T(1024)}, u32[]{:S(2)}) copy-start(f32[1536]{0:T(1024)} %copy-done.25) | copy-start | bytes 18436
  428.5 142.6 %copy-start.28 = (f32[1536]{0:T(1024)S(1)}, f32[1536]{0:T(1024)}, u32[]{:S(2)}) copy-start(f32[1536]{0:T(1024)} %copy-done.27) | copy-start | bytes 18436
  428.6 142.6 %copy-start.30 = (f32[1536]{0:T(1024)S(1)}, f32[1536]{0:T(1024)}, u32[]{:S(2)}) copy-start(f32[1536]{0:T(1024)} %copy-done.29) | copy-start | bytes 18436
  428.6 142.6 %copy-start.32 = (f32[1536]{0:T(1024)S(1)}, f32[1536]{0:T(1024)}, u32[]{:S(2)}) copy-start(f32[1536]{0:T(1024)} %copy-done.31) | copy-start | bytes 18436
  428.6 142.6 %copy-start.34 = (f32[1536]{0:T(1024)S(1)}, f32[1536]{0:T(1024)}, u32[]{:S(2)}) copy-start(f32[1536]{0:T(1024)} %copy-done.33) | copy-start | bytes 18436
  428.6 142.6 %copy-start.36 = (f32[1536]{0:T(1024)S(1)}, f32[1536]{0:T(1024)}, u32[]{:S(2)}) copy-start(f32[1536]{0:T(1024)} %copy-done.35) | copy-start | bytes 18436
  428.6 142.6 %copy-start.38 = (f32[1536]{0:T(1024)S(1)}, f32[1536]{0:T(1024)}, u32[]{:S(2)}) copy-start(f32[1536]{0:T(1024)} %copy-done.37) | copy-start | bytes 18436
  428.6 142.6 %copy-start.40 = (f32[1536]{0:T(1024)S(1)}, f32[1536]{0:T(1024)}, u32[]{:S(2)}) copy-start(f32[1536]{0:T(1024)} %copy-done.39) | copy-start | bytes 18436
  428.6 142.6 %copy-start.42 = (f32[1536]{0:T(1024)S(1)}, f32[1536]{0:T(1024)}, u32[]{:S(2)}) copy-start(f32[1536]{0:T(1024)} %copy-done.41) | copy-start | bytes 18436
  428.6 142.6 %copy-start.44 = (f32[1536]{0:T(1024)S(1)}, f32[1536]{0:T(1024)}, u32[]{:S(2)}) copy-start(f32[1536]{0:T(1024)} %copy-done.43) | copy-start | bytes 18436
  428.6 142.6 %copy-start.46 = (f32[1536]{0:T(1024)S(1)}, f32[1536]{0:T(1024)}, u32[]{:S(2)}) copy-start(f32[1536]{0:T(1024)} %copy-done.45) | copy-start | bytes 18436
  428.6 142.6 %copy-start.48 = (f32[1536]{0:T(1024)S(1)}, f32[1536]{0:T(1024)}, u32[]{:S(2)}) copy-start(f32[1536]{0:T(1024)} %copy-done.47) | copy-start | bytes 18436
  428.7 142.6 %copy-start.50 = (f32[1536]{0:T(1024)S(1)}, f32[1536]{0:T(1024)}, u32[]{:S(2)}) copy-start(f32[1536]{0:T(1024)} %copy-done.49) | copy-start | bytes 18436
  428.7 142.6 %copy-start.52 = (f32[1536]{0:T(1024)S(1)}, f32[1536]{0:T(1024)}, u32[]{:S(2)}) copy-start(f32[1536]{0:T(1024)} %copy-done.51) | copy-start | bytes 18436
  428.7 142.6 %copy-start.54 = (f32[1536]{0:T(1024)S(1)}, f32[1536]{0:T(1024)}, u32[]{:S(2)}) copy-start(f32[1536]{0:T(1024)} %copy-done.53) | copy-start | bytes 18436
  428.7 142.6 %copy-start.56 = (f32[1536]{0:T(1024)S(1)}, f32[1536]{0:T(1024)}, u32[]{:S(2)}) copy-start(f32[1536]{0:T(1024)} %copy-done.55) | copy-start | bytes 18436
  428.7 142.6 %copy-start.58 = (f32[1536]{0:T(1024)S(1)}, f32[1536]{0:T(1024)}, u32[]{:S(2)}) copy-start(f32[1536]{0:T(1024)} %copy-done.57) | copy-start | bytes 18436
  428.7 142.6 %copy-start.60 = (f32[1536]{0:T(1024)S(1)}, f32[1536]{0:T(1024)}, u32[]{:S(2)}) copy-start(f32[1536]{0:T(1024)} %copy-done.59) | copy-start | bytes 18436
  428.7 142.6 %copy-start.62 = (f32[1536]{0:T(1024)S(1)}, f32[1536]{0:T(1024)}, u32[]{:S(2)}) copy-start(f32[1536]{0:T(1024)} %copy-done.61) | copy-start | bytes 18436
  428.7 142.6 %copy-start.64 = (f32[1536]{0:T(1024)S(1)}, f32[1536]{0:T(1024)}, u32[]{:S(2)}) copy-start(f32[1536]{0:T(1024)} %copy-done.63) | copy-start | bytes 18436
  428.7 142.6 %copy-start.66 = (f32[1536]{0:T(1024)S(1)}, f32[1536]{0:T(1024)}, u32[]{:S(2)}) copy-start(f32[1536]{0:T(1024)} %copy-done.65) | copy-start | bytes 18436
  428.8 200.9 %all-reduce.5.cloned.1.call-start = ((), (), s32[]{:S(2)}) async-start(), calls=%async_computation.3 | async-start | bytes 196608 | tf_op jit(solution)/shard_map/psum | solution.py:120
  433.5 56.7 %collective-permute-start.1 = (bf16[2,15,1536]{2,1,0:T(8,128)(2,1)S(1)}, bf16[2,15,1536]{2,1,0:T(8,128)(2,1)S(1)}, u32[]{:S(2)}, u32[]{:S(2)}) collective-permute-start(bf16[2,15,1536]{2,1,0:T(8,128)(2,1)S(1)} %get-tuple-element.147), channel_id=1, source_target_pairs={{1,0},{2,1},{3,2},{4,3},{5,4},{6,5},{7,6},{8,7},{9,8},{10,9},{11,1... | collective-permute-start | bytes 276488 | tf_op jit(solution)/shard_map/ppermute | solution.py:19
  (15 other events, 175.0 us)
Sparse Core Ops, SparseCore 0:
  11.2 123.0 all-gather.2
  137.4 116.7 all-gather.4
  428.9 59.9 all-reduce.2
  492.6 137.0 all-reduce.4
